TPU v7x, 32 devices: a whole 2x2x4 slice. The times are simulated.
32 devices in a mesh: src: 8 (over z, x), tgt: 4 (over y, core).
Axes of the slice: x: 2, y: 2, z: 4, core: 2. Of those that a mesh axis runs over, the one named last changes fastest.
Arguments:
- src_emb: bfloat16 [64, 16384], P(None, 'src'), may hold values from -2.75 to 2.75
- tgt_emb: bfloat16 [64, 32768], P(None, 'tgt'), may hold values from -2.75 to 2.75
- target_features: bfloat16 [128, 32768], P(None, 'tgt'), may hold values from -6 to 6
- src_mass: float32 [16384], P('src'), may hold values from 1 to 10
- tgt_mass: float32 [32768], P('tgt'), may hold values from 1 to 10
- kept_blocks: int32 [64, 32], P('src', 'tgt'), may hold values from 0 to 31, as said below
- kept_count: int32 [64, 4], P('src', 'tgt'), may hold values from 1 to 8
Outputs:
- projected: float32 [16384, 128], P(('src', 'tgt'))
- src_potential: float32 [16384], P('src')
- tgt_potential: float32 [32768], P('tgt')
Inputs may be any that keep to these rules, and one draw needn't show every extreme that they name: `kept_blocks`: entry [r, t * 8 + k] is a block number within target shard t; the 8 entries of one group are distinct; the first kept_count[r, t] of them are kept, the others are unused; every target block is kept by some source block row.
All inputs are finite; a program needn't handle non-finite values.
Results may differ from a plain program's by a relative error of at most 0.00075.
Values sent between devices are 32-bit elements; how exact they have to be, the bound alone decides.
No kernel may reach another device: no remote copies, remote signals or barrier semaphores. Data moves between devices by JAX's collectives and lax.ppermute only.
A program may use at most 64 MiB of HBM per device.

v0:
```python
import jax
import jax.numpy as jnp
from jax import lax
from jax.sharding import PartitionSpec as P

BLOCK = 256
ITERS = 2


SENTINEL = -1e30
EPSILON = 0.1


def pair_distance(src_tile, norm_tile, tgt_chosen, tgt_norm_chosen):
    products = jnp.einsum("dr,dkc->krc", src_tile, tgt_chosen, preferred_element_type=jnp.float32)
    return norm_tile[None, :, None] + tgt_norm_chosen[:, None, :] - 2.0 * products


def merge_rows(highest, totals):
    overall = lax.pmax(highest, "tgt")
    return (overall, lax.psum(totals * jnp.exp(highest - overall), "tgt"))


def merge_columns(block_top, block_sum):
    overall = lax.pmax(block_top, "src")
    return (overall, lax.psum(block_sum * jnp.exp(block_top - overall), "src"))


def shards(src_emb, tgt_emb, target_features, src_mass, tgt_mass, kept_blocks, kept_count):
    emb_width = src_emb.shape[0]
    src_rows = src_emb.shape[1]
    tgt_rows = tgt_emb.shape[1]
    src_blocks = src_rows // BLOCK
    tgt_blocks = tgt_rows // BLOCK
    slot_count = kept_blocks.shape[1]
    src_tiles = src_emb.reshape(emb_width, src_blocks, BLOCK).transpose(1, 0, 2)
    src_norm = jnp.sum(jnp.square(src_emb.astype(jnp.float32)), axis=0).reshape(src_blocks, BLOCK)
    tgt_tiles = tgt_emb.reshape(emb_width, tgt_blocks, BLOCK)
    target_norm = jnp.sum(jnp.square(tgt_emb.astype(jnp.float32)), axis=0).reshape(
        tgt_blocks, BLOCK
    )
    feat_tiles = target_features.reshape(target_features.shape[0], tgt_blocks, BLOCK)
    live_slot = lax.broadcasted_iota(jnp.int32, (src_blocks, slot_count), 1) < kept_count
    packets = (src_tiles, src_norm, kept_blocks, live_slot)
    flat_index = kept_blocks.reshape(-1)
    member = (
        lax.broadcasted_iota(jnp.int32, (tgt_blocks, flat_index.shape[0]), 0) == flat_index[None, :]
    )

    def distances(packet):
        return pair_distance(
            packet[0],
            packet[1],
            jnp.take(tgt_tiles, packet[2], axis=1),
            jnp.take(target_norm, packet[2], axis=0),
        )

    def row_scaled(potential_tiles, packet):
        scaled = (
            jnp.take(potential_tiles, packet[2], axis=0)[:, None, :] - distances(packet)
        ) / EPSILON
        return jnp.where(packet[3][:, None, None], scaled, SENTINEL)

    tgt_potential = jnp.zeros((tgt_rows,), jnp.float32)
    src_potential = jnp.zeros((src_rows,), jnp.float32)
    for iteration in range(ITERS):
        row_potential_tiles = tgt_potential.reshape(tgt_blocks, BLOCK)

        def row_per_block(packet):
            scaled = row_scaled(row_potential_tiles, packet)
            highest = jnp.max(scaled, axis=(0, 2))
            totals = jnp.sum(
                jnp.where(packet[3][:, None, None], jnp.exp(scaled - highest[None, :, None]), 0.0),
                axis=(0, 2),
            )
            return (highest, totals)

        highest, totals = lax.map(row_per_block, packets)
        highest, totals = merge_rows(*(highest.reshape(src_rows), totals.reshape(src_rows)))
        src_potential = EPSILON * jnp.log(src_mass) - EPSILON * (highest + jnp.log(totals))
        column_potential_tiles = src_potential.reshape(src_blocks, BLOCK)

        def column_per_block(packet):
            scaled = (packet[4][None, :, None] - distances(packet)) / EPSILON
            scaled = jnp.where(packet[3][:, None, None], scaled, SENTINEL)
            highest = jnp.max(scaled, axis=1)
            totals = jnp.sum(
                jnp.where(packet[3][:, None, None], jnp.exp(scaled - highest[:, None, :]), 0.0),
                axis=1,
            )
            return (highest, totals)

        slot_top, slot_sum = lax.map(column_per_block, packets + (column_potential_tiles,))
        slot_top = slot_top.reshape(src_blocks * slot_count, BLOCK)
        slot_sum = slot_sum.reshape(src_blocks * slot_count, BLOCK)
        block_top = jnp.max(jnp.where(member[:, :, None], slot_top[None, :, :], SENTINEL), axis=1)
        scaled_sum = slot_sum * jnp.exp(slot_top - jnp.take(block_top, flat_index, axis=0))
        block_sum = jnp.dot(member.astype(jnp.float32), scaled_sum, precision=lax.Precision.HIGHEST)
        block_top, block_sum = merge_columns(
            *(block_top.reshape(tgt_rows), block_sum.reshape(tgt_rows))
        )
        tgt_potential = EPSILON * jnp.log(tgt_mass) - EPSILON * (block_top + jnp.log(block_sum))
    final_tiles = tgt_potential.reshape(tgt_blocks, BLOCK)

    def local_peak(packet):
        return jnp.max(row_scaled(final_tiles, packet), axis=(0, 2))

    local_top = lax.map(local_peak, packets)

    def weigh(packet):
        scaled = row_scaled(final_tiles, packet)
        weights = jnp.where(
            packet[3][:, None, None], jnp.exp(scaled - packet[4][None, :, None]), 0.0
        )
        rounded_count = lax.optimization_barrier(weights.astype(jnp.bfloat16))
        numerator = jnp.einsum(
            "krc,fkc->rf",
            rounded_count,
            jnp.take(feat_tiles, packet[2], axis=1),
            preferred_element_type=jnp.float32,
        )
        return (numerator, jnp.sum(rounded_count.astype(jnp.float32), axis=(0, 2)))

    numerator, denominator = lax.map(weigh, packets + (local_top,))
    numerator = numerator.reshape(src_rows, target_features.shape[0])
    denominator = denominator.reshape(src_rows)
    local_top = local_top.reshape(src_rows)
    overall = lax.pmax(local_top, "tgt")
    factor = jnp.exp(local_top - overall)
    numerator = numerator * factor[:, None]
    denominator = denominator * factor
    numerator, denominator = (
        lax.psum_scatter(numerator, "tgt", scatter_dimension=0, tiled=True),
        lax.psum_scatter(denominator, "tgt", scatter_dimension=0, tiled=True),
    )
    projected = numerator / denominator[:, None]
    return (projected, src_potential, tgt_potential)


def solution(mesh):
    return jax.shard_map(
        shards,
        mesh=mesh,
        in_specs=(
            P(None, "src"),
            P(None, "tgt"),
            P(None, "tgt"),
            P("src"),
            P("tgt"),
            P("src", "tgt"),
            P("src", "tgt"),
        ),
        out_specs=(P(("src", "tgt"), None), P("src"), P("tgt")),
        check_vma=False,
    )
```

profile of v0, /device:TPU:0, one launch (start us, length us, event | category | flops | bytes accessed | tf_op | source)
XLA Modules:
  0.0 395.9 jit_solution(6069955016342824660)
XLA Ops:
  11.3 26.2 %while.70 = (s32[]{:T(128)}, f32[8,256]{1,0:T(8,128)S(1)}, f32[8,256]{1,0:T(8,128)S(1)}, pred[8,8]{1,0:T(8,128)(4,1)S(1)}, s32[8,8]{1,0:T(8,128)S(1)}, /*index=5...) while((s32[]{:T(128)}, f32[8,256]{1,0:T(8,128)S(1)}, ...), condition=%wide.region_5.8_spmd, body=%wide.region_2.7_spmd.sunk | while | flops 72487472 | bytes 5143929 | solution.py:78
  37.5 8.5 %pmax.35 = f32[2048]{0:T(1024)S(1)} all-reduce(f32[2048]{0:T(1024)S(1)} %bitcast.349), channel_id=1, replica_groups=mesh['src'=8,'tgt'=4] {'tgt'}, use_global_device_ids=true, to_apply=%region_6.9 | all-reduce | flops 2048 | bytes 16384 | tf_op jit(solution)/shard_map/pmax | solution.py:20
  46.1 5.9 %psum.28 = f32[2048]{0:T(1024)S(1)} all-reduce(f32[2048]{0:T(1024)S(1)} %exponential_multiply_fusion.3), channel_id=1, replica_groups=mesh['src'=8,'tgt'=4] {'tgt'}, use_global_device_ids=true, to_apply=%region_7.10 | all-reduce | flops 2048 | bytes 16384 | tf_op jit(solution)/shard_map/psum | solution.py:21
  52.0 19.6 %while.71 = (s32[]{:T(128)}, f32[8,8,256]{2,1,0:T(8,128)S(1)}, f32[8,8,256]{2,1,0:T(8,128)S(1)}, pred[8,8]{1,0:T(8,128)(4,1)S(1)}, f32[8,256]{1,0:T(8,128)S(1)},...) while((s32[]{:T(128)}, f32[8,8,256]{2,1,0:T(8,128)S(1)}, ...), condition=%wide.region_11.14_spmd, body=%wide.region_8.13_spmd.sunk | while | flops 72481840 | bytes 5123405 | solution.py:93
  73.1 37.4 %pmax.36 = f32[8192]{0:T(1024)S(1)} all-reduce(f32[8192]{0:T(1024)S(1)} %bitcast.336), channel_id=1, replica_groups=mesh['src'=8,'tgt'=4] {'src'}, use_global_device_ids=true, to_apply=%region_13.16 | all-reduce | flops 8192 | bytes 65536 | tf_op jit(solution)/shard_map/pmax | solution.py:25
  110.6 33.0 %psum.29 = f32[8192]{0:T(1024)S(1)} all-reduce(f32[8192]{0:T(1024)S(1)} %exponential_multiply_fusion.1), channel_id=1, replica_groups=mesh['src'=8,'tgt'=4] {'src'}, use_global_device_ids=true, to_apply=%region_14.18 | all-reduce | flops 8192 | bytes 65536 | tf_op jit(solution)/shard_map/psum | solution.py:26
  143.6 26.1 %while.72 = (s32[]{:T(128)}, f32[8,256]{1,0:T(8,128)S(1)}, f32[8,256]{1,0:T(8,128)S(1)}, pred[8,8]{1,0:T(8,128)(4,1)S(1)}, s32[8,8]{1,0:T(8,128)S(1)}, /*index=5...) while((s32[]{:T(128)}, f32[8,256]{1,0:T(8,128)S(1)}, ...), condition=%wide.region_18.22_spmd, body=%wide.region_15.21_spmd.sunk | while | flops 72487472 | bytes 5111157 | solution.py:78
  169.8 5.9 %pmax.37 = f32[2048]{0:T(1024)S(1)} all-reduce(f32[2048]{0:T(1024)S(1)} %bitcast.351), channel_id=1, replica_groups=mesh['src'=8,'tgt'=4] {'tgt'}, use_global_device_ids=true, to_apply=%region_19.23 | all-reduce | flops 2048 | bytes 16384 | tf_op jit(solution)/shard_map/pmax | solution.py:20
  175.7 5.9 %psum.30 = f32[2048]{0:T(1024)S(1)} all-reduce(f32[2048]{0:T(1024)S(1)} %exponential_multiply_fusion.2), channel_id=1, replica_groups=mesh['src'=8,'tgt'=4] {'tgt'}, use_global_device_ids=true, to_apply=%region_20.24 | all-reduce | flops 2048 | bytes 16384 | tf_op jit(solution)/shard_map/psum | solution.py:21
  182.2 19.6 %while.73 = (s32[]{:T(128)}, f32[8,8,256]{2,1,0:T(8,128)S(1)}, f32[8,8,256]{2,1,0:T(8,128)S(1)}, pred[8,8]{1,0:T(8,128)(4,1)S(1)}, f32[8,256]{1,0:T(8,128)S(1)},...) while((s32[]{:T(128)}, f32[8,8,256]{2,1,0:T(8,128)S(1)}, ...), condition=%wide.region_24.28_spmd, body=%wide.region_21.27_spmd.sunk | while | flops 72481840 | bytes 5123405 | solution.py:93
  203.2 33.0 %pmax.38 = f32[8192]{0:T(1024)S(1)} all-reduce(f32[8192]{0:T(1024)S(1)} %bitcast.338), channel_id=1, replica_groups=mesh['src'=8,'tgt'=4] {'src'}, use_global_device_ids=true, to_apply=%region_26.30 | all-reduce | flops 8192 | bytes 65536 | tf_op jit(solution)/shard_map/pmax | solution.py:25
  236.3 33.2 %psum.31 = f32[8192]{0:T(1024)S(1)} all-reduce(f32[8192]{0:T(1024)S(1)} %exponential_multiply_fusion), channel_id=1, replica_groups=mesh['src'=8,'tgt'=4] {'src'}, use_global_device_ids=true, to_apply=%region_27.31 | all-reduce | flops 8192 | bytes 65536 | tf_op jit(solution)/shard_map/psum | solution.py:26
  270.1 24.3 %while.74 = (s32[]{:T(128)}, f32[8,256]{1,0:T(8,128)S(1)}, pred[8,8]{1,0:T(8,128)(4,1)S(1)}, s32[8,8]{1,0:T(8,128)S(1)}, f32[32,256]{1,0:T(8,128)S(1)}, /*index=...) while((s32[]{:T(128)}, f32[8,256]{1,0:T(8,128)S(1)}, ...), condition=%wide.region_30.34_spmd, body=%wide.region_28.33_spmd.sunk | while | flops 70914864 | bytes 912737 | solution.py:108
  294.4 3.2 copy.66
  297.6 2.9 copy.69
  300.6 55.7 %while.75 = (s32[]{:T(128)}, f32[8,256,128]{2,1,0:T(8,128)}, f32[8,256]{1,0:T(8,128)S(1)}, pred[8,8]{1,0:T(8,128)(4,1)S(1)}, s32[8,8]{1,0:T(8,128)S(1)}, /*index...) while((s32[]{:T(128)}, f32[8,256,128]{2,1,0:T(8,128)}, ...), condition=%wide.region_33.37_spmd, body=%wide.region_31.36_spmd.sunk | while | flops 207492928 | bytes 5770245 | solution.py:124
  303.8 2.2 gather_fusion.16
  317.8 2.2 gather_fusion.16
  324.7 2.2 gather_fusion.16
  352.6 2.2 gather_fusion.16
  356.3 5.8 %pmax.39 = f32[2048]{0:T(1024)S(1)} all-reduce(f32[2048]{0:T(1024)S(1)} %bitcast.347), channel_id=1, replica_groups=mesh['src'=8,'tgt'=4] {'tgt'}, use_global_device_ids=true, to_apply=%region_34.38 | all-reduce | flops 2048 | bytes 16384 | tf_op jit(solution)/shard_map/pmax | solution.py:128
  362.1 2.6 bitcast_multiply_fusion
  366.0 6.8 %all-reduce = f32[2048]{0:T(1024)S(1)} all-reduce(f32[2048]{0:T(1024)S(1)} %get-tuple-element.706), channel_id=3, replica_groups=mesh['src'=8,'tgt'=4] {'tgt'}, use_global_device_ids=true, to_apply=%region_36.40.clone | all-reduce | flops 2048 | bytes 16384
  372.8 14.4 %reduce-scatter.2.cloned.1.call-done = f32[512,128]{1,0:T(8,128)} async-done(((f32[2048,128]{1,0:T(8,128)}), f32[512,128]{1,0:T(8,128)}) %reduce-scatter.2.cloned.1.call-update) | async-done | bytes 262160 | tf_op jit(solution)/shard_map/reduce_scatter | solution.py:133
  (646 shorter events, 169.8 us)
Async XLA Ops:
  7.2 3.8 copy-start
  7.2 380.1 %reduce-scatter.2.cloned.1.call-start = ((), (), s32[]{:S(2)}) async-start(), calls=%async_computation.1 | async-start | bytes 1310720 | tf_op jit(solution)/shard_map/reduce_scatter | solution.py:133
  8.1 3.1 copy-start.6
  8.1 3.2 copy-start.3
  11.3 40.7 %copy-start.5 = (f32[2048]{0:T(1024)S(1)}, f32[2048]{0:T(1024)}, u32[]{:S(2)}) copy-start(f32[2048]{0:T(1024)} %param.28) | copy-start | bytes 24580
  52.0 91.6 %copy-start.2 = (f32[8192]{0:T(1024)S(1)}, f32[8192]{0:T(1024)}, u32[]{:S(2)}) copy-start(f32[8192]{0:T(1024)} %param.29) | copy-start | bytes 98308
  181.6 0.6 copy-start.4
  269.5 0.6 copy-start.1
  356.3 8.4 %copy-start.7 = (u32[32]{0:T(128)S(1)}, u32[32]{0:T(128)}, u32[]{:S(2)}) copy-start(u32[32]{0:T(128)} %constant.200) | copy-start | bytes 388
Sparse Core Ops, SparseCore 0:
  364.8 22.3 reduce-scatter.1
where the time goes:
time: 397 us; the launch traced here: 396 us
  blocking collectives  175 us (44%)
  local copies, waits for them, and re-layouts  104 us (26%)
  matrix products  55.5 us (14%)
  other arithmetic  27.4 us (7%)
  between operations  15.2 us (4%)
  waiting for transfers between devices  14.5 us (4%)
    pmax x2, blocking collectives, merge_columns(): overall = lax.pmax(block_top, 'src')  70.5 us
    psum x2, blocking collectives, merge_columns(): return (overall, lax.psum(block_sum * jnp.exp(block_top - overall), 'src'))  66.2 us
    dot_general x48, matrix products, pair_distance(): jnp.einsum('dr,dkc->krc', src_tile, tgt_chosen, preferred_element_type=jn...  45.6 us
    gather x48, local copies, waits for them, and re-layouts, distances(): jnp.take(target_norm, packet[2], axis=0)  27 us
    gather x48, local copies, waits for them, and re-layouts, distances(): jnp.take(tgt_tiles, packet[2], axis=1)  27 us
    gather x32, local copies, waits for them, and re-layouts, row_scaled(): jnp.take(potential_tiles, packet[2], axis=0)[:, None, :] - distances(packet)  18 us
    gather x8, local copies, waits for them, and re-layouts, weigh(): jnp.take(feat_tiles, packet[2], axis=1)  17.4 us
    reduce_scatter x1, waiting for transfers between devices, shards(): lax.psum_scatter(numerator, 'tgt', scatter_dimension=0, tiled=True)  14.4 us
  transfers between devices with their start and end apart: 1, of which 1 were waited for; matrix products, arithmetic and copies ran while one was open for 0% of the time, Pallas kernels for 0%

commit v1 on v0

--- a/solution.py
+++ b/solution.py
@@ -16,14 +16,63 @@
     return norm_tile[None, :, None] + tgt_norm_chosen[:, None, :] - 2.0 * products
 
 
+def lse_pair(top, total, other_top, other_total):
+    overall = jnp.maximum(top, other_top)
+    return (overall, total * jnp.exp(top - overall) + other_total * jnp.exp(other_top - overall))
+
+
+def butterfly_lse(highest, totals, axis):
+    size = lax.axis_size(axis)
+    step = 1
+    while step < size:
+        pairs = [(i, i ^ step) for i in range(size)]
+        other = lax.ppermute(jnp.stack([highest, totals]), axis, pairs)
+        highest, totals = lse_pair(highest, totals, other[0], other[1])
+        step *= 2
+    return (highest, totals)
+
+
 def merge_rows(highest, totals):
-    overall = lax.pmax(highest, "tgt")
-    return (overall, lax.psum(totals * jnp.exp(highest - overall), "tgt"))
+    return butterfly_lse(highest, totals, "tgt")
 
 
 def merge_columns(block_top, block_sum):
-    overall = lax.pmax(block_top, "src")
-    return (overall, lax.psum(block_sum * jnp.exp(block_top - overall), "src"))
+    return butterfly_lse(block_top, block_sum, "src")
+
+
+def halving_merge(top, numerator, denominator, axis):
+    size = lax.axis_size(axis)
+    me = lax.axis_index(axis)
+    rows = top.shape[0] // size
+    top = top.reshape(size, rows)
+    denominator = denominator.reshape(size, rows)
+    numerator = numerator.reshape(size, rows, numerator.shape[-1])
+    step = 1
+    while step < size:
+        pairs = [(i, i ^ step) for i in range(size)]
+        keep = (me // step) % 2
+        count = top.shape[0] // 2
+
+        def split(x):
+            x = x.reshape((count, 2) + x.shape[1:])
+            return (
+                lax.dynamic_index_in_dim(x, keep, axis=1, keepdims=False),
+                lax.dynamic_index_in_dim(x, 1 - keep, axis=1, keepdims=False),
+            )
+
+        top_keep, top_send = split(top)
+        den_keep, den_send = split(denominator)
+        num_keep, num_send = split(numerator)
+        small = lax.ppermute(jnp.stack([top_send, den_send]), axis, pairs)
+        num_other = lax.ppermute(num_send, axis, pairs)
+        overall = jnp.maximum(top_keep, small[0])
+        mine = jnp.exp(top_keep - overall)
+        theirs = jnp.exp(small[0] - overall)
+        numerator = num_keep * mine[..., None] + num_other * theirs[..., None]
+        denominator = den_keep * mine + small[1] * theirs
+        top = overall
+        step *= 2
+    return (numerator.reshape(rows, -1), denominator.reshape(rows))
 
 
 def shards(src_emb, tgt_emb, target_features, src_mass, tgt_mass, kept_blocks, kept_count):
@@ -125,14 +174,7 @@
     numerator = numerator.reshape(src_rows, target_features.shape[0])
     denominator = denominator.reshape(src_rows)
     local_top = local_top.reshape(src_rows)
-    overall = lax.pmax(local_top, "tgt")
-    factor = jnp.exp(local_top - overall)
-    numerator = numerator * factor[:, None]
-    denominator = denominator * factor
-    numerator, denominator = (
-        lax.psum_scatter(numerator, "tgt", scatter_dimension=0, tiled=True),
-        lax.psum_scatter(denominator, "tgt", scatter_dimension=0, tiled=True),
-    )
+    numerator, denominator = halving_merge(local_top, numerator, denominator, "tgt")
     projected = numerator / denominator[:, None]
     return (projected, src_potential, tgt_potential)
 

time: 397 us -> 243 us (0.61)
  blocking collectives: 175 us -> 0 us
  starting transfers between devices: 0.04 us -> 21.7 us
  between operations: 15.2 us -> 1.3 us
  waiting for transfers between devices: 14.5 us -> 25.9 us
    pmax x5 -> x0, blocking collectives: 90.6 us -> none  [the longest x2 70.5 us: merge_columns(): overall = lax.pmax(block_top, 'src')]
    psum x4 -> x0, blocking collectives: 78 us -> none  [the longest x2 66.2 us: merge_columns(): return (overall, lax.psum(block_sum * jnp.exp(block_top - overall), 'src'))]
    ppermute x0 -> x14, waiting for transfers between devices: none -> 25.9 us  [the longest x10 18.1 us: butterfly_lse(): other = lax.ppermute(jnp.stack([highest, totals]), axis, pairs)]
    ppermute x0 -> x14, starting transfers between devices: none -> 21.7 us  [the longest x10 19 us: butterfly_lse(): other = lax.ppermute(jnp.stack([highest, totals]), axis, pairs)]
    reduce_scatter x1 -> x0, waiting for transfers between devices: 14.4 us -> none  [shards(): lax.psum_scatter(numerator, 'tgt', scatter_dimension=0, tiled=True)]
    unnamed x1 -> x0, blocking collectives: 6.77 us -> none
  transfers between devices with their start and end apart: 1 -> 14, of which waited for: 1 -> 11; matrix products, arithmetic and copies ran while one was open for 0% -> 3% of each run, Pallas kernels for 0% -> 0%
where the time goes in v1:
time: 243 us
  local copies, waits for them, and re-layouts  105 us (43%)
  matrix products  55.4 us (23%)
  other arithmetic  29.1 us (12%)
  waiting for transfers between devices  25.9 us (11%)
  starting transfers between devices  21.7 us (9%)
  loops' own time  3.9 us (2%)
    dot_general x48, matrix products, pair_distance(): jnp.einsum('dr,dkc->krc', src_tile, tgt_chosen, preferred_element_type=jn...  45.5 us
    gather x48, local copies, waits for them, and re-layouts, distances(): jnp.take(target_norm, packet[2], axis=0)  27 us
    gather x48, local copies, waits for them, and re-layouts, distances(): jnp.take(tgt_tiles, packet[2], axis=1)  27 us
    ppermute x10, starting transfers between devices, butterfly_lse(): other = lax.ppermute(jnp.stack([highest, totals]), axis, pairs)  19 us
    ppermute x10, waiting for transfers between devices, butterfly_lse(): other = lax.ppermute(jnp.stack([highest, totals]), axis, pairs)  18.1 us
    gather x32, local copies, waits for them, and re-layouts, row_scaled(): jnp.take(potential_tiles, packet[2], axis=0)[:, None, :] - distances(packet)  18 us
    gather x8, local copies, waits for them, and re-layouts, weigh(): jnp.take(feat_tiles, packet[2], axis=1)  17.4 us
    dot_general x8, matrix products, weigh(): jnp.einsum('krc,fkc->rf', rounded_count, jnp.take(feat_tiles, packet[2],...  9.43 us
  transfers between devices with their start and end apart: 14, of which 11 were waited for; matrix products, arithmetic and copies ran while one was open for 3% of the time, Pallas kernels for 0%

profile of v1, /device:TPU:0, one launch (start us, length us, event | category | flops | bytes accessed | tf_op | source)
XLA Modules:
  0.0 242.6 jit_solution(2462594371334962322)
XLA Ops:
  3.9 26.2 %while.70 = (s32[]{:T(128)}, f32[8,256]{1,0:T(8,128)S(1)}, f32[8,256]{1,0:T(8,128)S(1)}, pred[8,8]{1,0:T(8,128)(4,1)S(1)}, s32[8,8]{1,0:T(8,128)S(1)}, /*index=5...) while((s32[]{:T(128)}, f32[8,256]{1,0:T(8,128)S(1)}, ...), condition=%wide.region_5.8_spmd, body=%wide.region_2.7_spmd.sunk | while | flops 72487472 | bytes 5143929 | solution.py:127
  31.6 2.9 %collective-permute-start.1 = (f32[2,2048]{1,0:T(2,128)S(1)}, f32[2,2048]{1,0:T(2,128)S(1)}, u32[]{:S(2)}, u32[]{:S(2)}) collective-permute-start(f32[2,2048]{1,0:T(2,128)S(1)} %pad_maximum_fusion.7), channel_id=1, source_target_pairs={{0,2},{1,3},{2,0},{3,1},{4,6},{5,7},{6,4},{7,5},{8,10},{9,11},{10,... | collective-permute-start | bytes 49160 | tf_op jit(solution)/shard_map/ppermute | solution.py:29
  36.3 19.5 %while.71 = (s32[]{:T(128)}, f32[8,8,256]{2,1,0:T(8,128)S(1)}, f32[8,8,256]{2,1,0:T(8,128)S(1)}, pred[8,8]{1,0:T(8,128)(4,1)S(1)}, f32[8,256]{1,0:T(8,128)S(1)},...) while((s32[]{:T(128)}, f32[8,8,256]{2,1,0:T(8,128)S(1)}, ...), condition=%wide.region_9.12_spmd, body=%wide.region_6.11_spmd.sunk | while | flops 72481840 | bytes 5123405 | solution.py:142
  59.5 2.3 collective-permute-done.2
  64.1 2.2 collective-permute-done.3
  66.6 3.6 %collective-permute-start.4 = (f32[2,8192]{1,0:T(2,128)S(1)}, f32[2,8192]{1,0:T(2,128)S(1)}, u32[]{:S(2)}, u32[]{:S(2)}) collective-permute-start(f32[2,8192]{1,0:T(2,128)S(1)} %pad_maximum_fusion.2), channel_id=1, source_target_pairs={{0,16},{4,20},{8,24},{12,28},{16,0},{20,4},{24,8},{28,12},{1,17},{... | collective-permute-start | bytes 196616 | tf_op jit(solution)/shard_map/ppermute | solution.py:29
  70.3 2.2 collective-permute-done.4
  72.6 26.1 %while.72 = (s32[]{:T(128)}, f32[8,256]{1,0:T(8,128)S(1)}, f32[8,256]{1,0:T(8,128)S(1)}, pred[8,8]{1,0:T(8,128)(4,1)S(1)}, s32[8,8]{1,0:T(8,128)S(1)}, /*index=5...) while((s32[]{:T(128)}, f32[8,256]{1,0:T(8,128)S(1)}, ...), condition=%wide.region_14.18_spmd, body=%wide.region_11.17_spmd.sunk | while | flops 72487472 | bytes 5111157 | solution.py:127
  101.8 2.2 collective-permute-done.6
  104.6 19.5 %while.73 = (s32[]{:T(128)}, f32[8,8,256]{2,1,0:T(8,128)S(1)}, f32[8,8,256]{2,1,0:T(8,128)S(1)}, pred[8,8]{1,0:T(8,128)(4,1)S(1)}, f32[8,256]{1,0:T(8,128)S(1)},...) while((s32[]{:T(128)}, f32[8,8,256]{2,1,0:T(8,128)S(1)}, ...), condition=%wide.region_18.22_spmd, body=%wide.region_15.21_spmd.sunk | while | flops 72481840 | bytes 5123405 | solution.py:142
  127.3 2.8 %collective-permute-done.7 = f32[2,8192]{1,0:T(2,128)S(1)} collective-permute-done((f32[2,8192]{1,0:T(2,128)S(1)}, f32[2,8192]{1,0:T(2,128)S(1)}, u32[]{:S(2)}, u32[]{:S(2)}) %collective-permute-start.7) | collective-permute-done | bytes 65568 | tf_op jit(solution)/shard_map/ppermute | solution.py:29
  132.3 2.9 %collective-permute-done.8 = f32[2,8192]{1,0:T(2,128)S(1)} collective-permute-done((f32[2,8192]{1,0:T(2,128)S(1)}, f32[2,8192]{1,0:T(2,128)S(1)}, u32[]{:S(2)}, u32[]{:S(2)}) %collective-permute-start.8) | collective-permute-done | bytes 65568 | tf_op jit(solution)/shard_map/ppermute | solution.py:29
  136.5 3.0 %collective-permute-start.9 = (f32[2,8192]{1,0:T(2,128)}, f32[2,8192]{1,0:T(2,128)}, u32[]{:S(2)}, u32[]{:S(2)}) collective-permute-start(f32[2,8192]{1,0:T(2,128)} %pad_maximum_fusion.5), channel_id=1, source_target_pairs={{0,16},{4,20},{8,24},{12,28},{16,0},{20,4},{24,8},{28,12},{1,17},{... | collective-permute-start | bytes 196616 | tf_op jit(solution)/shard_map/ppermute | solution.py:29
  139.6 3.2 %copy.57 = bf16[128,8192]{0,1:T(8,128)(2,1)S(1)} copy(bf16[128,8192]{1,0:T(8,128)(2,1)} %param.27) | data formatting | bytes 4194304 | tf_op args[2]
  142.8 2.9 %copy.60 = bf16[128,32,256]{2,0,1:T(8,128)(2,1)} copy(bf16[128,32,256]{0,2,1:T(8,128)(2,1)S(1)} %bitcast.432) | data formatting | bytes 4194304 | tf_op jit(solution)/shard_map/while | solution.py:173
  148.2 24.3 %while.74 = (s32[]{:T(128)}, f32[8,256]{1,0:T(8,128)S(1)}, pred[8,8]{1,0:T(8,128)(4,1)S(1)}, s32[8,8]{1,0:T(8,128)S(1)}, f32[32,256]{1,0:T(8,128)S(1)}, /*index=...) while((s32[]{:T(128)}, f32[8,256]{1,0:T(8,128)S(1)}, ...), condition=%wide.region_22.26_spmd, body=%wide.region_20.25_spmd.sunk | while | flops 70914864 | bytes 912737 | solution.py:157
  172.5 55.9 %while.75 = (s32[]{:T(128)}, f32[8,256,128]{2,1,0:T(8,128)}, f32[8,256]{1,0:T(8,128)S(1)}, pred[8,8]{1,0:T(8,128)(4,1)S(1)}, s32[8,8]{1,0:T(8,128)S(1)}, /*index...) while((s32[]{:T(128)}, f32[8,256,128]{2,1,0:T(8,128)}, ...), condition=%wide.region_25.29_spmd, body=%wide.region_23.28_spmd.sunk | while | flops 207492928 | bytes 5770245 | solution.py:173
  176.0 2.2 gather_fusion.16
  183.0 2.2 gather_fusion.16
  189.9 2.2 gather_fusion.16
  210.8 2.2 gather_fusion.16
  217.8 2.2 gather_fusion.16
  224.7 2.2 gather_fusion.16
  235.2 6.4 %collective-permute-done.12 = f32[2,1,512]{2,1,0:T(1,128)S(1)} collective-permute-done((f32[2,1,512]{2,1,0:T(1,128)S(1)}, f32[2,1,512]{2,1,0:T(1,128)S(1)}, u32[]{:S(2)}, u32[]{:S(2)}) %collective-permute-start.12) | collective-permute-done | bytes 4128 | tf_op jit(solution)/shard_map/ppermute | solution.py:66
  (691 shorter events, 187.7 us)
Async XLA Ops:
  0.6 2.9 %copy-start = (bf16[64,2048]{1,0:T(8,128)(2,1)S(1)}, bf16[64,2048]{1,0:T(8,128)(2,1)}, u32[]{:S(2)}) copy-start(bf16[64,2048]{1,0:T(8,128)(2,1)} %param.25) | copy-start | bytes 786436
  0.6 3.1 %copy-start.6 = (s32[8,1]{0,1:T(1,128)S(1)}, s32[8,1]{0,1:T(1,128)}, u32[]{:S(2)}) copy-start(s32[8,1]{0,1:T(1,128)} %param.31) | copy-start | bytes 100
  0.7 3.2 %copy-start.3 = (s32[8,8]{1,0:T(8,128)S(1)}, s32[8,8]{1,0:T(8,128)}, u32[]{:S(2)}) copy-start(s32[8,8]{1,0:T(8,128)} %param.30) | copy-start | bytes 772
  3.9 32.4 %copy-start.5 = (f32[2048]{0:T(1024)S(1)}, f32[2048]{0:T(1024)}, u32[]{:S(2)}) copy-start(f32[2048]{0:T(1024)} %param.28) | copy-start | bytes 24580
  30.2 1.4 collective-permute-start
  31.6 4.6 %collective-permute-start.1 = (f32[2,2048]{1,0:T(2,128)S(1)}, f32[2,2048]{1,0:T(2,128)S(1)}, u32[]{:S(2)}, u32[]{:S(2)}) collective-permute-start(f32[2,2048]{1,0:T(2,128)S(1)} %pad_maximum_fusion.7), channel_id=1, source_target_pairs={{0,2},{1,3},{2,0},{3,1},{4,6},{5,7},{6,4},{7,5},{8,10},{9,11},{10,... | collective-permute-start | bytes 49160 | tf_op jit(solution)/shard_map/ppermute | solution.py:29
  55.9 16.6 %copy-start.1 = (f32[8192]{0:T(1024)S(1)}, f32[8192]{0:T(1024)}, u32[]{:S(2)}) copy-start(f32[8192]{0:T(1024)} %param.29) | copy-start | bytes 98308
  57.5 4.3 %collective-permute-start.2 = (f32[2,8192]{1,0:T(2,128)S(1)}, f32[2,8192]{1,0:T(2,128)S(1)}, u32[]{:S(2)}, u32[]{:S(2)}) collective-permute-start(f32[2,8192]{1,0:T(2,128)S(1)} %pad_maximum_fusion), channel_id=1, source_target_pairs={{0,4},{4,0},{8,12},{12,8},{16,20},{20,16},{24,28},{28,24},{1,5},{5... | collective-permute-start | bytes 196616 | tf_op jit(solution)/shard_map/ppermute | solution.py:29
  62.0 4.4 %collective-permute-start.3 = (f32[2,8192]{1,0:T(2,128)S(1)}, f32[2,8192]{1,0:T(2,128)S(1)}, u32[]{:S(2)}, u32[]{:S(2)}) collective-permute-start(f32[2,8192]{1,0:T(2,128)S(1)} %pad_maximum_fusion.1), channel_id=1, source_target_pairs={{0,8},{4,12},{8,0},{12,4},{16,24},{20,28},{24,16},{28,20},{1,9},{5... | collective-permute-start | bytes 196616 | tf_op jit(solution)/shard_map/ppermute | solution.py:29
  66.6 5.9 %collective-permute-start.4 = (f32[2,8192]{1,0:T(2,128)S(1)}, f32[2,8192]{1,0:T(2,128)S(1)}, u32[]{:S(2)}, u32[]{:S(2)}) collective-permute-start(f32[2,8192]{1,0:T(2,128)S(1)} %pad_maximum_fusion.2), channel_id=1, source_target_pairs={{0,16},{4,20},{8,24},{12,28},{16,0},{20,4},{24,8},{28,12},{1,17},{... | collective-permute-start | bytes 196616 | tf_op jit(solution)/shard_map/ppermute | solution.py:29
  98.8 1.2 collective-permute-start.5
  100.1 3.8 %collective-permute-start.6 = (f32[2,2048]{1,0:T(2,128)S(1)}, f32[2,2048]{1,0:T(2,128)S(1)}, u32[]{:S(2)}, u32[]{:S(2)}) collective-permute-start(f32[2,2048]{1,0:T(2,128)S(1)} %pad_maximum_fusion.9), channel_id=1, source_target_pairs={{0,2},{1,3},{2,0},{3,1},{4,6},{5,7},{6,4},{7,5},{8,10},{9,11},{10,... | collective-permute-start | bytes 49160 | tf_op jit(solution)/shard_map/ppermute | solution.py:29
  104.0 0.6 copy-start.4
  125.7 4.3 %collective-permute-start.7 = (f32[2,8192]{1,0:T(2,128)S(1)}, f32[2,8192]{1,0:T(2,128)S(1)}, u32[]{:S(2)}, u32[]{:S(2)}) collective-permute-start(f32[2,8192]{1,0:T(2,128)S(1)} %pad_maximum_fusion.3), channel_id=1, source_target_pairs={{0,4},{4,0},{8,12},{12,8},{16,20},{20,16},{24,28},{28,24},{1,5},{5... | collective-permute-start | bytes 196616 | tf_op jit(solution)/shard_map/ppermute | solution.py:29
  130.8 4.3 %collective-permute-start.8 = (f32[2,8192]{1,0:T(2,128)S(1)}, f32[2,8192]{1,0:T(2,128)S(1)}, u32[]{:S(2)}, u32[]{:S(2)}) collective-permute-start(f32[2,8192]{1,0:T(2,128)S(1)} %pad_maximum_fusion.4), channel_id=1, source_target_pairs={{0,8},{4,12},{8,0},{12,4},{16,24},{20,28},{24,16},{28,20},{1,9},{5... | collective-permute-start | bytes 196616 | tf_op jit(solution)/shard_map/ppermute | solution.py:29
  136.5 9.2 %collective-permute-start.9 = (f32[2,8192]{1,0:T(2,128)}, f32[2,8192]{1,0:T(2,128)}, u32[]{:S(2)}, u32[]{:S(2)}) collective-permute-start(f32[2,8192]{1,0:T(2,128)} %pad_maximum_fusion.5), channel_id=1, source_target_pairs={{0,16},{4,20},{8,24},{12,28},{16,0},{20,4},{24,8},{28,12},{1,17},{... | collective-permute-start | bytes 196616 | tf_op jit(solution)/shard_map/ppermute | solution.py:29
  147.6 0.6 copy-start.2
  229.6 2.0 collective-permute-start.11
  229.7 1.9 collective-permute-start.10
  233.1 8.5 %collective-permute-start.13 = (f32[1,512,128]{2,1,0:T(8,128)S(1)}, f32[1,512,128]{2,1,0:T(8,128)S(1)}, u32[]{:S(2)}, u32[]{:S(2)}) collective-permute-start(f32[1,512,128]{2,1,0:T(8,128)S(1)} %constant_dynamic-slice_fusion.16), channel_id=1, source_target_pairs={{0,2},{1,3},{2,0},{3,1},{4,6},{5,7},{6,4},{7,5},{8,10},{9,11},{10,... | collective-permute-start | bytes 786440 | tf_op jit(solution)/shard_map/ppermute | solution.py:67
  234.7 6.9 %collective-permute-start.12 = (f32[2,1,512]{2,1,0:T(1,128)S(1)}, f32[2,1,512]{2,1,0:T(1,128)S(1)}, u32[]{:S(2)}, u32[]{:S(2)}) collective-permute-start(f32[2,1,512]{2,1,0:T(1,128)S(1)} %pad_maximum_fusion.11), channel_id=1, source_target_pairs={{0,2},{1,3},{2,0},{3,1},{4,6},{5,7},{6,4},{7,5},{8,10},{9,11},{10,... | collective-permute-start | bytes 12296 | tf_op jit(solution)/shard_map/ppermute | solution.py:66
